TPU v7x, 32 devices: a whole 2x2x4 slice. The times are simulated.
32 devices in a mesh: groups: 2 (over y), lon: 4 (over z), chan: 2 (over x), lat: 2 (over core).
Axes of the slice: x: 2, y: 2, z: 4, core: 2. Of those that a mesh axis runs over, the one named last changes fastest.
Arguments:
- inputs: bfloat16 [256, 64, 512], P('chan', ('groups', 'lat'), 'lon'), parts along dimension 1, may hold values from -6 to 6
- cotangent: bfloat16 [256, 64, 512], P('chan', ('groups', 'lat'), 'lon'), parts along dimension 1, may hold values from -6 to 6
- weight: bfloat16 [3, 3, 256, 256], P(None, None, 'chan'), may hold values from -0.125 to 0.125
- bias_vector: float32 [256], P('chan'), may hold values from -4 to 4
Outputs:
- input_grad: bfloat16 [256, 64, 512], P('chan', ('groups', 'lat'), 'lon'), parts along dimension 1
- weight_grad: float32 [6, 3, 256, 256], P('groups', None, 'chan'), parts along dimension 0
- bias_grad: float32 [512], P(('groups', 'chan')), parts along dimension 0
There are 2 independent parts, one for each index of `groups`. A program takes and returns all parts, laid end to end along the dimension named above; an argument that names none is the same for every part. Nothing has to cross between parts.
All inputs are finite; a program needn't handle non-finite values.
Results may differ from a plain program's by a relative error of at most 0.007.
Values may be sent and summed in bfloat16 or wider, within the bound.
No kernel may reach another device: no remote copies, remote signals or barrier semaphores. Data moves between devices by JAX's collectives and lax.ppermute only.
A program may use at most 64 MiB of HBM per device.

v0:
```python
import jax
import jax.numpy as jnp
from jax import lax
from jax.sharding import PartitionSpec as P


def padded_2(shard, sides, width):
    for axis, dim in sides:
        devices, length = (lax.axis_size(axis), shard.shape[dim])
        up = [(i, (i + 1) % devices) for i in range(devices)]
        down = [(j, i) for i, j in up]
        last = lax.slice_in_dim(shard, length - width, length, axis=dim)
        initial = lax.slice_in_dim(shard, 0, width, axis=dim)
        before = lax.ppermute(last, axis, up)
        after = lax.ppermute(initial, axis, down)
        shard = jnp.concatenate([before, shard, after], axis=dim)
    return shard


def gelu_slope(preact):
    normal_cdf = 0.5 * (1.0 + jax.scipy.special.erf(preact * 0.7071067811865476))
    density = jnp.exp(-0.5 * preact * preact) * 0.3989422804014327
    return normal_cdf + preact * density


def mask_rims(padded):
    lat_index = lax.axis_index("lat")
    band_count = lax.axis_size("lat")
    row_ids = jnp.arange(padded.shape[1])
    outside = (row_ids == 0) & (lat_index == 0) | (row_ids == padded.shape[1] - 1) & (
        lat_index == band_count - 1
    )
    return jnp.where(outside[None, :, None], jnp.zeros((), padded.dtype), padded)


def window_of(field, first_row, first_col, row_count, column_count):
    return field[
        :, first_row : first_row + row_count, first_col : first_col + column_count
    ].reshape(field.shape[0], -1)


def local(inputs, cotangent, weight, bias_vector):
    own_channels, row_count, column_count = inputs.shape
    input_pad = mask_rims(padded_2(inputs, (("lon", 2), ("lat", 1)), 1))
    input_all = lax.all_gather(input_pad, "chan", axis=0, tiled=True)
    preact = jnp.zeros((own_channels, row_count * column_count), jnp.float32)
    for tap_row in range(3):
        for tap_col in range(3):
            window = window_of(input_all, tap_row, tap_col, row_count, column_count)
            preact = preact + jnp.dot(
                weight[tap_row, tap_col], window, preferred_element_type=jnp.float32
            )
    preact = preact + bias_vector[:, None]
    upstream = cotangent.reshape(own_channels, -1).astype(jnp.float32)
    grad_pre = (upstream * gelu_slope(preact)).astype(jnp.bfloat16)
    bias_part = jnp.sum(grad_pre.astype(jnp.float32), axis=1)
    taps = []
    for tap_row in range(3):
        row_taps = []
        for tap_col in range(3):
            window = window_of(input_all, tap_row, tap_col, row_count, column_count)
            row_taps.append(
                lax.dot_general(
                    grad_pre, window, (((1,), (1,)), ((), ())), preferred_element_type=jnp.float32
                )
            )
        taps.append(jnp.stack(row_taps))
    weight_part = jnp.stack(taps)
    weight_grad, bias_grad = lax.psum((weight_part, bias_part), ("lon", "lat"))
    grad_field = grad_pre.reshape(own_channels, row_count, column_count)
    grad_pad = mask_rims(padded_2(grad_field, (("lon", 2), ("lat", 1)), 1))
    amount = lax.axis_size("chan") * own_channels
    summed = jnp.zeros((amount, row_count * column_count), jnp.float32)
    for tap_row in range(3):
        for tap_col in range(3):
            kernel_cols = weight[tap_row, tap_col]
            window = window_of(grad_pad, 2 - tap_row, 2 - tap_col, row_count, column_count)
            summed = summed + lax.dot_general(
                kernel_cols, window, (((0,), (0,)), ((), ())), preferred_element_type=jnp.float32
            )
    input_sum = lax.psum_scatter(
        summed.reshape(amount, row_count, column_count), "chan", scatter_dimension=0, tiled=True
    )
    return (input_sum.astype(jnp.bfloat16), weight_grad, bias_grad)


def solution(mesh):
    placed = (
        P("chan", ("groups", "lat"), "lon"),
        P("chan", ("groups", "lat"), "lon"),
        P(None, None, "chan", None),
        P("chan"),
    )
    return jax.shard_map(
        local,
        mesh=mesh,
        in_specs=placed,
        out_specs=(
            P("chan", ("groups", "lat"), "lon"),
            P("groups", None, "chan", None),
            P(("groups", "chan")),
        ),
        check_vma=False,
    )
```

profile of v0, /device:TPU:0, one launch (start us, length us, event | category | flops | bytes accessed | tf_op | source)
XLA Modules:
  0.0 177.4 jit_solution(9235394544272731963)
XLA Ops:
  7.2 0.0 all-gather.2.cloned.1.call-start
  7.2 1.5 copy.13
  8.8 3.1 %collective-permute-start = (bf16[128,16,1]{0,2,1:T(2,128)(2,1)S(1)}, bf16[128,16,1]{0,2,1:T(2,128)(2,1)S(1)}, u32[]{:S(2)}, u32[]{:S(2)}) collective-permute-start(bf16[128,16,1]{0,2,1:T(2,128)(2,1)S(1)} %get-tuple-element.27), channel_id=1, source_target_pairs={{0,4},{4,8},{8,12},{12,0},{1,5},{5,9},{9,13},{13,1},{2,6},{6,10},{... | collective-permute-start | bytes 12296 | tf_op jit(solution)/shard_map/ppermute | solution.py:14
  11.8 2.1 %collective-permute-start.1 = (bf16[128,16,1]{0,2,1:T(2,128)(2,1)S(1)}, bf16[128,16,1]{0,2,1:T(2,128)(2,1)S(1)}, u32[]{:S(2)}, u32[]{:S(2)}) collective-permute-start(bf16[128,16,1]{0,2,1:T(2,128)(2,1)S(1)} %get-tuple-element.28), channel_id=1, source_target_pairs={{4,0},{8,4},{12,8},{0,12},{5,1},{9,5},{13,9},{1,13},{6,2},{10,6},{... | collective-permute-start | bytes 12296 | tf_op jit(solution)/shard_map/ppermute | solution.py:15
  13.9 1.6 collective-permute-done
  15.6 0.1 collective-permute-start.2
  15.7 0.5 collective-permute-start.3
  16.2 0.7 collective-permute-done.2
  16.9 0.2 collective-permute-done.3
  17.0 1.1 maximum_select_fusion
  18.2 0.0 reduce-scatter.2.cloned.1.call-start
  18.2 1.4 copy.12
  19.6 23.9 %all-gather.2.cloned.1.call-done = bf16[256,18,130]{0,2,1:T(8,128)(2,1)} async-done(((bf16[128,18,130]{0,2,1:T(8,128)(2,1)}), bf16[256,18,130]{0,2,1:T(8,128)(2,1)}) %all-gather.2.cloned.1.call-update) | async-done | bytes 1198096 | tf_op jit(solution)/shard_map/all_gather | solution.py:45
  43.5 8.3 %fusion.46 = (bf16[256,16,128]{0,2,1:T(8,128)(2,1)S(1)}, bf16[256,16,128]{0,2,1:T(8,128)(2,1)S(1)}, bf16[256,16,128]{0,2,1:T(8,128)(2,1)S(1)}, bf16[256,16,128]{...) fusion(bf16[256,18,130]{0,2,1:T(8,128)(2,1)} %all-gather.2.clon, ...), kind=kLoop, calls=%fused_computation.86 | loop fusion | bytes 18874368 | tf_op jit(solution)/shard_map/slice | solution.py:37
  51.9 0.4 fusion.26
  52.3 0.4 convolution_add_fusion.15
  52.8 0.1 copy-done
  52.9 0.4 convolution_add_fusion.14
  53.3 0.4 convolution_add_fusion.13
  53.7 0.4 convolution_add_fusion.12
  54.2 0.4 convolution_add_fusion.11
  54.6 0.4 convolution_add_fusion.10
  55.1 0.4 convolution_add_fusion.9
  55.6 0.7 copy-done.13
  56.3 0.7 convert_reduce_fusion
  57.1 1.5 collective-permute-start.4
  58.6 2.3 %collective-permute-start.5 = (bf16[128,16,1]{0,2,1:T(2,128)(2,1)S(1)}, bf16[128,16,1]{0,2,1:T(2,128)(2,1)S(1)}, u32[]{:S(2)}, u32[]{:S(2)}) collective-permute-start(bf16[128,16,1]{0,2,1:T(2,128)(2,1)S(1)} %get-tuple-element.26), channel_id=1, source_target_pairs={{4,0},{8,4},{12,8},{0,12},{5,1},{9,5},{13,9},{1,13},{6,2},{10,6},{... | collective-permute-start | bytes 12296 | tf_op jit(solution)/shard_map/ppermute | solution.py:15
  60.9 1.6 collective-permute-done.4
  62.6 0.1 collective-permute-start.6
  62.7 0.5 collective-permute-start.7
  63.2 0.7 collective-permute-done.6
  63.9 0.2 collective-permute-done.7
  64.0 0.3 maximum_select_fusion.1
  64.4 0.9 fusion.47
  65.3 0.4 fusion.24
  65.7 0.4 convolution_add_fusion.7
  66.1 0.4 convolution_add_fusion.6
  66.6 0.4 convolution_add_fusion.5
  67.0 0.4 convolution_add_fusion.4
  67.4 0.4 convolution_add_fusion.3
  67.8 0.4 convolution_add_fusion.2
  68.2 0.4 convolution_add_fusion.1
  68.6 1.7 convolution_add_fusion
  70.4 3.0 %copy.16 = f32[256,16,128]{2,1,0:T(8,128)} copy(f32[256,16,128]{0,2,1:T(8,128)} %bitcast.154) | data formatting | bytes 4194304 | tf_op jit(solution)/shard_map/reshape | solution.py:82
  73.4 0.2 all-reduce.2.cloned.1.call-start
  73.6 1.7 convolution_bitcast_fusion
  75.3 1.7 convolution_bitcast_fusion.1
  77.0 0.4 convolution_bitcast_fusion.2
  77.4 0.4 convolution_bitcast_fusion.3
  77.8 0.4 copy-done.5
  78.2 0.4 convolution_bitcast_fusion.4
  78.6 0.1 copy-done.3
  78.7 0.4 convolution_bitcast_fusion.5
  79.0 0.5 copy-done.1
  79.5 0.4 convolution_bitcast_fusion.6
  79.9 0.3 convolution_bitcast_fusion.7
  80.2 0.3 convolution_bitcast_fusion.8
  80.6 0.1 maximum_bitcast_fusion
  80.6 1.1 pad_maximum_fusion
  81.8 17.9 %psum.15 = f32[128]{0:T(128)} all-reduce(f32[128]{0:T(128)S(1)} %get-tuple-element.29), channel_id=1, replica_groups=mesh['groups'=2,'lon'=4,'chan'=2,'lat'=2] {'lon','lat'}, use_global_device_ids=true, to_apply=%region_3.4 | all-reduce | flops 128 | bytes 1024 | tf_op jit(solution)/shard_map/psum | solution.py:69
  99.6 6.3 %reduce-scatter.2.cloned.1.call-done = f32[128,16,128]{2,1,0:T(8,128)} async-done(((f32[256,16,128]{2,1,0:T(8,128)}), f32[128,16,128]{2,1,0:T(8,128)}) %reduce-scatter.2.cloned.1.call-update) | async-done | bytes 1048592 | tf_op jit(solution)/shard_map/reduce_scatter | solution.py:81
  105.9 2.1 %convert_element_type.18 = bf16[128,16,128]{2,1,0:T(8,128)(2,1)} convert(f32[128,16,128]{2,1,0:T(8,128)} %reduce-scatter.2.cloned.1.call-done) | non-fusion elementwise | flops 262144 | bytes 1572864 | tf_op jit(solution)/shard_map/convert_element_type | solution.py:84
  108.0 60.5 %all-reduce.2.cloned.1.call-done = f32[3,3,128,256]{3,2,1,0:T(8,128)} async-done(((f32[3,3,128,256]{3,2,1,0:T(8,128)}), f32[3,3,128,256]{3,2,1,0:T(8,128)}) %all-reduce.2.cloned.1.call-update) | async-done | bytes 1179664 | tf_op jit(solution)/shard_map/psum | solution.py:69
  168.5 2.4 %copy.18 = f32[3,3,128,256]{3,2,1,0:T(8,128)} copy(f32[3,3,128,256]{3,2,1,0:T(8,128)} %all-reduce.2.cloned.1.call-done) | data formatting | bytes 2359296
  (38 shorter events, 0.2 us)
Async XLA Ops:
  7.2 11.1 %copy-start.14 = (bf16[128,16,128]{2,1,0:T(8,128)(2,1)S(1)}, bf16[128,16,128]{2,1,0:T(8,128)(2,1)}, u32[]{:S(2)}) copy-start(bf16[128,16,128]{2,1,0:T(8,128)(2,1)} %param.5) | copy-start | bytes 1572868
  7.2 36.3 %all-gather.2.cloned.1.call-start = ((), (), s32[]{:S(2)}) async-start(), calls=%async_computation.1 | async-start | bytes 1880064 | tf_op jit(solution)/shard_map/all_gather | solution.py:45
  8.8 6.8 %collective-permute-start = (bf16[128,16,1]{0,2,1:T(2,128)(2,1)S(1)}, bf16[128,16,1]{0,2,1:T(2,128)(2,1)S(1)}, u32[]{:S(2)}, u32[]{:S(2)}) collective-permute-start(bf16[128,16,1]{0,2,1:T(2,128)(2,1)S(1)} %get-tuple-element.27), channel_id=1, source_target_pairs={{0,4},{4,8},{8,12},{12,0},{1,5},{5,9},{9,13},{13,1},{2,6},{6,10},{... | collective-permute-start | bytes 12296 | tf_op jit(solution)/shard_map/ppermute | solution.py:14
  11.8 3.7 %collective-permute-start.1 = (bf16[128,16,1]{0,2,1:T(2,128)(2,1)S(1)}, bf16[128,16,1]{0,2,1:T(2,128)(2,1)S(1)}, u32[]{:S(2)}, u32[]{:S(2)}) collective-permute-start(bf16[128,16,1]{0,2,1:T(2,128)(2,1)S(1)} %get-tuple-element.28), channel_id=1, source_target_pairs={{4,0},{8,4},{12,8},{0,12},{5,1},{9,5},{13,9},{1,13},{6,2},{10,6},{... | collective-permute-start | bytes 12296 | tf_op jit(solution)/shard_map/ppermute | solution.py:15
  15.6 1.3 collective-permute-start.2
  15.7 1.4 collective-permute-start.3
  18.2 87.8 %reduce-scatter.2.cloned.1.call-start = ((), (), s32[]{:S(2)}) async-start(), calls=%async_computation.2 | async-start | bytes 3145728 | tf_op jit(solution)/shard_map/reduce_scatter | solution.py:81
  19.6 32.3 %copy-start.12 = (bf16[3,3,128,256]{3,2,1,0:T(8,128)(2,1)S(1)}, bf16[3,3,128,256]{3,2,1,0:T(8,128)(2,1)}, u32[]{:S(2)}) copy-start(bf16[3,3,128,256]{3,2,1,0:T(8,128)(2,1)} %param.6) | copy-start | bytes 1769476
  51.8 1.0 copy-start
  51.9 1.4 copy-start.2
  51.9 1.9 %copy-start.4 = (bf16[256,16,128]{0,2,1:T(8,128)(2,1)}, bf16[256,16,128]{0,2,1:T(8,128)(2,1)S(1)}, u32[]{:S(2)}) copy-start(bf16[256,16,128]{0,2,1:T(8,128)(2,1)S(1)} %get-tuple-element.7) | copy-start | bytes 3145732
  51.9 2.3 %copy-start.6 = (bf16[256,16,128]{0,2,1:T(8,128)(2,1)}, bf16[256,16,128]{0,2,1:T(8,128)(2,1)S(1)}, u32[]{:S(2)}) copy-start(bf16[256,16,128]{0,2,1:T(8,128)(2,1)S(1)} %get-tuple-element.6) | copy-start | bytes 3145732
  51.9 2.7 %copy-start.8 = (bf16[256,16,128]{0,2,1:T(8,128)(2,1)}, bf16[256,16,128]{0,2,1:T(8,128)(2,1)S(1)}, u32[]{:S(2)}) copy-start(bf16[256,16,128]{0,2,1:T(8,128)(2,1)S(1)} %get-tuple-element.5) | copy-start | bytes 3145732
  51.9 3.2 %copy-start.10 = (bf16[256,16,128]{0,2,1:T(8,128)(2,1)}, bf16[256,16,128]{0,2,1:T(8,128)(2,1)S(1)}, u32[]{:S(2)}) copy-start(bf16[256,16,128]{0,2,1:T(8,128)(2,1)S(1)} %get-tuple-element.4) | copy-start | bytes 3145732
  51.9 3.6 %copy-start.11 = (bf16[256,16,128]{0,2,1:T(8,128)(2,1)}, bf16[256,16,128]{0,2,1:T(8,128)(2,1)S(1)}, u32[]{:S(2)}) copy-start(bf16[256,16,128]{0,2,1:T(8,128)(2,1)S(1)} %get-tuple-element.3) | copy-start | bytes 3145732
  55.1 1.2 copy-start.13
  55.1 1.2 copy-start.15
  57.1 5.5 %collective-permute-start.4 = (bf16[128,16,1]{0,2,1:T(2,128)(2,1)S(1)}, bf16[128,16,1]{0,2,1:T(2,128)(2,1)S(1)}, u32[]{:S(2)}, u32[]{:S(2)}) collective-permute-start(bf16[128,16,1]{0,2,1:T(2,128)(2,1)S(1)} %get-tuple-element.25), channel_id=1, source_target_pairs={{0,4},{4,8},{8,12},{12,0},{1,5},{5,9},{9,13},{13,1},{2,6},{6,10},{... | collective-permute-start | bytes 12296 | tf_op jit(solution)/shard_map/ppermute | solution.py:14
  58.6 4.0 %collective-permute-start.5 = (bf16[128,16,1]{0,2,1:T(2,128)(2,1)S(1)}, bf16[128,16,1]{0,2,1:T(2,128)(2,1)S(1)}, u32[]{:S(2)}, u32[]{:S(2)}) collective-permute-start(bf16[128,16,1]{0,2,1:T(2,128)(2,1)S(1)} %get-tuple-element.26), channel_id=1, source_target_pairs={{4,0},{8,4},{12,8},{0,12},{5,1},{9,5},{13,9},{1,13},{6,2},{10,6},{... | collective-permute-start | bytes 12296 | tf_op jit(solution)/shard_map/ppermute | solution.py:15
  62.6 1.3 collective-permute-start.6
  62.7 1.4 collective-permute-start.7
  73.4 95.1 %all-reduce.2.cloned.1.call-start = ((), (), s32[]{:S(2)}) async-start(), calls=%async_computation.3 | async-start | bytes 2359296 | tf_op jit(solution)/shard_map/psum | solution.py:69
  73.6 3.3 %copy-start.9 = (bf16[256,16,128]{0,2,1:T(8,128)(2,1)S(1)}, bf16[256,16,128]{0,2,1:T(8,128)(2,1)}, u32[]{:S(2)}) copy-start(bf16[256,16,128]{0,2,1:T(8,128)(2,1)} %copy-done.8) | copy-start | bytes 3145732
  75.3 2.1 %copy-start.7 = (bf16[256,16,128]{0,2,1:T(8,128)(2,1)S(1)}, bf16[256,16,128]{0,2,1:T(8,128)(2,1)}, u32[]{:S(2)}) copy-start(bf16[256,16,128]{0,2,1:T(8,128)(2,1)} %copy-done.6) | copy-start | bytes 3145732
  77.0 1.2 copy-start.5
  77.4 1.3 copy-start.3
  78.2 1.3 copy-start.1
Sparse Core Ops, SparseCore 0:
  18.3 25.1 all-gather.1
  73.5 32.3 reduce-scatter.1
  109.0 59.5 all-reduce.1
where the time goes:
time: 178 us; the launch traced here: 177 us
  waiting for transfers between devices  95.8 us (54%)
  local copies, waits for them, and re-layouts  19.5 us (11%)
  blocking collectives  17.9 us (10%)
  matrix products  15 us (8%)
  between operations  14.2 us (8%)
  starting transfers between devices  10.5 us (6%)
  other arithmetic  4.73 us (3%)
    psum x1, waiting for transfers between devices, local(): weight_grad, bias_grad = lax.psum((weight_part, bias_part), ('lon', 'lat'))  60.5 us
    all_gather x1, waiting for transfers between devices, local(): input_all = lax.all_gather(input_pad, 'chan', axis=0, tiled=True)  23.9 us
    psum x1, blocking collectives, local(): weight_grad, bias_grad = lax.psum((weight_part, bias_part), ('lon', 'lat'))  17.9 us
    slice x2, local copies, waits for them, and re-layouts, window_of(): field[:, first_row:first_row + row_count, first_col:first_col + column_co...  9.24 us
    reduce_scatter x1, waiting for transfers between devices, local(): lax.psum_scatter(summed.reshape(amount, row_count, column_count), 'chan',...  6.31 us
    unnamed x34, local copies, waits for them, and re-layouts  5.76 us
    dot_general x9, matrix products, local(): lax.dot_general(grad_pre, window, (((1,), (1,)), ((), ())), preferred_ele...  5.76 us
    ppermute x4, starting transfers between devices, padded_2(): after = lax.ppermute(initial, axis, down)  5.42 us
  transfers between devices with their start and end apart: 11, of which 9 were waited for; matrix products, arithmetic and copies ran while one was open for 6% of the time, Pallas kernels for 0%

commit v1 on v0

--- a/solution.py
+++ b/solution.py
@@ -1,7 +1,17 @@
+import functools
 import jax
 import jax.numpy as jnp
 from jax import lax
 from jax.sharding import PartitionSpec as P
+
+
+def _take_strips_all(t0, link_axis, named_axis):
+    then = lax.psum(t0, link_axis)
+    y_new = lax.psum(then, named_axis)
+    return y_new
+
+
+arrange_wall_on = functools.partial(_take_strips_all, link_axis="lat", named_axis="lon")
 
 
 def padded_2(shard, sides, width):
@@ -66,7 +76,7 @@
             )
         taps.append(jnp.stack(row_taps))
     weight_part = jnp.stack(taps)
-    weight_grad, bias_grad = lax.psum((weight_part, bias_part), ("lon", "lat"))
+    weight_grad, bias_grad = arrange_wall_on((weight_part, bias_part))
     grad_field = grad_pre.reshape(own_channels, row_count, column_count)
     grad_pad = mask_rims(padded_2(grad_field, (("lon", 2), ("lat", 1)), 1))
     amount = lax.axis_size("chan") * own_channels

time: 178 us -> 190 us (1.067)
  waiting for transfers between devices: 95.8 us -> 119 us
  matrix products: 15 us -> 11.1 us
  local copies, waits for them, and re-layouts: 19.5 us -> 15.8 us
  blocking collectives: 17.9 us -> 14.9 us
    reduce_scatter x1, waiting for transfers between devices: 6.31 us -> 20.5 us  [local(): lax.psum_scatter(summed.reshape(amount, row_count, column_count), 'chan',...]
    psum x1 -> x2, waiting for transfers between devices: 60.5 us -> 69.1 us  [the longest x1 56.1 us: _take_strips_all(): y_new = lax.psum(then, named_axis)]
    psum x1 -> x2, blocking collectives: 17.9 us -> 14.9 us  [the longest x1 12.4 us: _take_strips_all(): y_new = lax.psum(then, named_axis)]
    dot_general x9, matrix products: 5.76 us -> 3.19 us  [local(): lax.dot_general(grad_pre, window, (((1,), (1,)), ((), ())), preferred_ele...]
    unnamed x34 -> x8, local copies, waits for them, and re-layouts: 5.76 us -> 4.1 us
  transfers between devices with their start and end apart: 11 -> 12, of which waited for: 9 -> 8; matrix products, arithmetic and copies ran while one was open for 6% -> 6% of each run, Pallas kernels for 0% -> 0%
where the time goes in v1:
time: 190 us
  waiting for transfers between devices  119 us (63%)
  local copies, waits for them, and re-layouts  15.8 us (8%)
  blocking collectives  14.9 us (8%)
  between operations  14.1 us (7%)
  matrix products  11.1 us (6%)
  starting transfers between devices  10.5 us (6%)
  other arithmetic  4.7 us (2%)
    psum x1, waiting for transfers between devices, _take_strips_all(): y_new = lax.psum(then, named_axis)  56.1 us
    all_gather x1, waiting for transfers between devices, local(): input_all = lax.all_gather(input_pad, 'chan', axis=0, tiled=True)  24.8 us
    reduce_scatter x1, waiting for transfers between devices, local(): lax.psum_scatter(summed.reshape(amount, row_count, column_count), 'chan',...  20.5 us
    psum x1, waiting for transfers between devices, _take_strips_all(): then = lax.psum(t0, link_axis)  13.1 us
    psum x1, blocking collectives, _take_strips_all(): y_new = lax.psum(then, named_axis)  12.4 us
    slice x2, local copies, waits for them, and re-layouts, window_of(): field[:, first_row:first_row + row_count, first_col:first_col + column_co...  9.2 us
    ppermute x4, starting transfers between devices, padded_2(): after = lax.ppermute(initial, axis, down)  5.41 us
    ppermute x4, starting transfers between devices, padded_2(): before = lax.ppermute(last, axis, up)  4.77 us
  transfers between devices with their start and end apart: 12, of which 8 were waited for; matrix products, arithmetic and copies ran while one was open for 6% of the time, Pallas kernels for 0%

profile of v1, /device:TPU:0, one launch (start us, length us, event | category | flops | bytes accessed | tf_op | source)
XLA Modules:
  0.0 189.7 jit_solution(6016607692126858154)
XLA Ops:
  7.2 0.0 all-gather.2.cloned.1.call-start
  7.2 1.5 copy.13
  8.8 3.1 %collective-permute-start = (bf16[128,16,1]{0,2,1:T(2,128)(2,1)S(1)}, bf16[128,16,1]{0,2,1:T(2,128)(2,1)S(1)}, u32[]{:S(2)}, u32[]{:S(2)}) collective-permute-start(bf16[128,16,1]{0,2,1:T(2,128)(2,1)S(1)} %get-tuple-element.27), channel_id=1, source_target_pairs={{0,4},{4,8},{8,12},{12,0},{1,5},{5,9},{9,13},{13,1},{2,6},{6,10},{... | collective-permute-start | bytes 12296 | tf_op jit(solution)/shard_map/ppermute | solution.py:24
  11.8 2.1 %collective-permute-start.1 = (bf16[128,16,1]{0,2,1:T(2,128)(2,1)S(1)}, bf16[128,16,1]{0,2,1:T(2,128)(2,1)S(1)}, u32[]{:S(2)}, u32[]{:S(2)}) collective-permute-start(bf16[128,16,1]{0,2,1:T(2,128)(2,1)S(1)} %get-tuple-element.28), channel_id=1, source_target_pairs={{4,0},{8,4},{12,8},{0,12},{5,1},{9,5},{13,9},{1,13},{6,2},{10,6},{... | collective-permute-start | bytes 12296 | tf_op jit(solution)/shard_map/ppermute | solution.py:25
  13.9 1.6 collective-permute-done
  15.6 0.1 collective-permute-start.2
  15.7 0.5 collective-permute-start.3
  16.2 0.7 collective-permute-done.2
  16.9 0.2 collective-permute-done.3
  17.0 1.1 maximum_select_fusion
  18.1 0.0 all-gather.2.cloned.1.call-update
  18.1 0.0 all-reduce.3.cloned.1.call-start
  18.2 0.4 copy.12
  18.7 24.8 %all-gather.2.cloned.1.call-done = bf16[256,18,130]{0,2,1:T(8,128)(2,1)} async-done(((bf16[128,18,130]{0,2,1:T(8,128)(2,1)}), bf16[256,18,130]{0,2,1:T(8,128)(2,1)}) %all-gather.2.cloned.1.call-update) | async-done | bytes 1198096 | tf_op jit(solution)/shard_map/all_gather | solution.py:55
  43.5 8.3 %fusion.46 = (bf16[256,16,128]{0,2,1:T(8,128)(2,1)S(1)}, bf16[256,16,128]{0,2,1:T(8,128)(2,1)S(1)}, bf16[256,16,128]{0,2,1:T(8,128)(2,1)S(1)}, bf16[256,16,128]{...) fusion(bf16[256,18,130]{0,2,1:T(8,128)(2,1)} %all-gather.2.clon, ...), kind=kLoop, calls=%fused_computation.86 | loop fusion | bytes 18874368 | tf_op jit(solution)/shard_map/slice | solution.py:47
  51.8 0.4 fusion.26
  52.2 0.4 convolution_add_fusion.15
  52.6 0.4 convolution_add_fusion.14
  53.1 0.4 convolution_add_fusion.13
  53.5 0.4 convolution_add_fusion.12
  54.0 0.4 convolution_add_fusion.11
  54.4 0.4 convolution_add_fusion.10
  54.8 0.4 convolution_add_fusion.9
  55.3 0.2 copy-done.2
  55.5 0.7 convert_reduce_fusion
  56.2 0.4 convolution_bitcast_fusion
  56.6 0.4 convolution_bitcast_fusion.1
  57.0 0.4 convolution_bitcast_fusion.2
  57.3 0.4 convolution_bitcast_fusion.3
  57.7 0.4 convolution_bitcast_fusion.4
  58.0 0.4 convolution_bitcast_fusion.5
  58.4 0.4 convolution_bitcast_fusion.6
  58.8 0.4 convolution_bitcast_fusion.7
  59.1 0.4 convolution_bitcast_fusion.8
  59.5 1.6 collective-permute-start.4
  61.1 2.3 %collective-permute-start.5 = (bf16[128,16,1]{0,2,1:T(2,128)(2,1)S(1)}, bf16[128,16,1]{0,2,1:T(2,128)(2,1)S(1)}, u32[]{:S(2)}, u32[]{:S(2)}) collective-permute-start(bf16[128,16,1]{0,2,1:T(2,128)(2,1)S(1)} %get-tuple-element.26), channel_id=1, source_target_pairs={{4,0},{8,4},{12,8},{0,12},{5,1},{9,5},{13,9},{1,13},{6,2},{10,6},{... | collective-permute-start | bytes 12296 | tf_op jit(solution)/shard_map/ppermute | solution.py:25
  63.4 0.1 maximum_bitcast_fusion
  63.5 1.5 collective-permute-done.4
  65.1 0.1 collective-permute-start.6
  65.1 0.5 collective-permute-start.7
  65.6 1.1 pad_maximum_fusion
  66.7 0.2 reduce-scatter.2.cloned.1.call-start
  67.0 0.3 maximum_select_fusion.1
  67.3 0.9 fusion.47
  68.2 0.4 fusion.24
  68.7 0.4 convolution_add_fusion.7
  69.1 0.4 convolution_add_fusion.6
  69.5 0.4 convolution_add_fusion.5
  69.9 0.4 convolution_add_fusion.4
  70.4 0.4 convolution_add_fusion.3
  70.8 0.4 convolution_add_fusion.2
  71.2 0.4 convolution_add_fusion.1
  71.6 0.4 convolution_add_fusion
  72.1 2.0 %copy.16 = f32[256,16,128]{2,1,0:T(8,128)} copy(f32[256,16,128]{0,2,1:T(8,128)S(1)} %bitcast.154) | data formatting | bytes 4194304 | tf_op jit(solution)/shard_map/reshape | solution.py:92
  74.1 0.0 reduce-scatter.2.cloned.1.call-update
  74.1 0.0 all-reduce.5.cloned.1.call-start
  74.1 13.1 %all-reduce.3.cloned.1.call-done = f32[3,3,128,256]{3,2,1,0:T(8,128)} async-done(((f32[3,3,128,256]{3,2,1,0:T(8,128)}), f32[3,3,128,256]{3,2,1,0:T(8,128)}) %all-reduce.3.cloned.1.call-update) | async-done | bytes 1179664 | tf_op jit(solution)/shard_map/psum | solution.py:9
  87.2 0.0 all-reduce.5.cloned.1.call-update
  87.2 2.5 %psum.30 = f32[128]{0:T(128)S(1)} all-reduce(f32[128]{0:T(128)S(1)} %get-tuple-element.29), channel_id=1, replica_groups=mesh['groups'=2,'lon'=4,'chan'=2,'lat'=2] {'lat'}, use_global_device_ids=true, to_apply=%region_4.5 | all-reduce | flops 128 | bytes 1024 | tf_op jit(solution)/shard_map/psum | solution.py:9
  89.7 12.4 %psum.31 = f32[128]{0:T(128)} all-reduce(f32[128]{0:T(128)S(1)} %psum.30), channel_id=1, replica_groups=mesh['groups'=2,'lon'=4,'chan'=2,'lat'=2] {'lon'}, use_global_device_ids=true, to_apply=%region_5.6 | all-reduce | flops 128 | bytes 1024 | tf_op jit(solution)/shard_map/psum | solution.py:10
  102.1 20.5 %reduce-scatter.2.cloned.1.call-done = f32[128,16,128]{2,1,0:T(8,128)} async-done(((f32[256,16,128]{2,1,0:T(8,128)}), f32[128,16,128]{2,1,0:T(8,128)}) %reduce-scatter.2.cloned.1.call-update) | async-done | bytes 1048592 | tf_op jit(solution)/shard_map/reduce_scatter | solution.py:91
  122.6 2.1 %convert_element_type.18 = bf16[128,16,128]{2,1,0:T(8,128)(2,1)} convert(f32[128,16,128]{2,1,0:T(8,128)} %reduce-scatter.2.cloned.1.call-done) | non-fusion elementwise | flops 262144 | bytes 1572864 | tf_op jit(solution)/shard_map/convert_element_type | solution.py:94
  124.7 56.1 %all-reduce.5.cloned.1.call-done = f32[3,3,128,256]{3,2,1,0:T(8,128)} async-done(((f32[3,3,128,256]{3,2,1,0:T(8,128)}), f32[3,3,128,256]{3,2,1,0:T(8,128)}) %all-reduce.5.cloned.1.call-update) | async-done | bytes 1179664 | tf_op jit(solution)/shard_map/psum | solution.py:10
  180.8 2.4 %copy.19 = f32[3,3,128,256]{3,2,1,0:T(8,128)} copy(f32[3,3,128,256]{3,2,1,0:T(8,128)} %all-reduce.5.cloned.1.call-done) | data formatting | bytes 2359296
  (16 shorter events, 0.2 us)
Async XLA Ops:
  7.2 11.0 %copy-start.1 = (bf16[128,16,128]{2,1,0:T(8,128)(2,1)S(1)}, bf16[128,16,128]{2,1,0:T(8,128)(2,1)}, u32[]{:S(2)}) copy-start(bf16[128,16,128]{2,1,0:T(8,128)(2,1)} %param.5) | copy-start | bytes 1572868
  7.2 36.3 %all-gather.2.cloned.1.call-start = ((), (), s32[]{:S(2)}) async-start(), calls=%async_computation.1 | async-start | bytes 1880064 | tf_op jit(solution)/shard_map/all_gather | solution.py:55
  8.8 6.8 %collective-permute-start = (bf16[128,16,1]{0,2,1:T(2,128)(2,1)S(1)}, bf16[128,16,1]{0,2,1:T(2,128)(2,1)S(1)}, u32[]{:S(2)}, u32[]{:S(2)}) collective-permute-start(bf16[128,16,1]{0,2,1:T(2,128)(2,1)S(1)} %get-tuple-element.27), channel_id=1, source_target_pairs={{0,4},{4,8},{8,12},{12,0},{1,5},{5,9},{9,13},{13,1},{2,6},{6,10},{... | collective-permute-start | bytes 12296 | tf_op jit(solution)/shard_map/ppermute | solution.py:24
  11.8 3.7 %collective-permute-start.1 = (bf16[128,16,1]{0,2,1:T(2,128)(2,1)S(1)}, bf16[128,16,1]{0,2,1:T(2,128)(2,1)S(1)}, u32[]{:S(2)}, u32[]{:S(2)}) collective-permute-start(bf16[128,16,1]{0,2,1:T(2,128)(2,1)S(1)} %get-tuple-element.28), channel_id=1, source_target_pairs={{4,0},{8,4},{12,8},{0,12},{5,1},{9,5},{13,9},{1,13},{6,2},{10,6},{... | collective-permute-start | bytes 12296 | tf_op jit(solution)/shard_map/ppermute | solution.py:25
  15.6 1.3 collective-permute-start.2
  15.7 1.4 collective-permute-start.3
  18.1 69.1 %all-reduce.3.cloned.1.call-start = ((), (), s32[]{:S(2)}) async-start(), calls=%async_computation.3 | async-start | bytes 2359296 | tf_op jit(solution)/shard_map/psum | solution.py:9
  18.6 33.1 %copy-start = (bf16[3,3,128,256]{3,2,1,0:T(8,128)(2,1)S(1)}, bf16[3,3,128,256]{3,2,1,0:T(8,128)(2,1)}, u32[]{:S(2)}) copy-start(bf16[3,3,128,256]{3,2,1,0:T(8,128)(2,1)} %param.6) | copy-start | bytes 1769476
  54.8 0.7 copy-start.2
  59.5 5.5 %collective-permute-start.4 = (bf16[128,16,1]{0,2,1:T(2,128)(2,1)S(1)}, bf16[128,16,1]{0,2,1:T(2,128)(2,1)S(1)}, u32[]{:S(2)}, u32[]{:S(2)}) collective-permute-start(bf16[128,16,1]{0,2,1:T(2,128)(2,1)S(1)} %get-tuple-element.25), channel_id=1, source_target_pairs={{0,4},{4,8},{8,12},{12,0},{1,5},{5,9},{9,13},{13,1},{2,6},{6,10},{... | collective-permute-start | bytes 12296 | tf_op jit(solution)/shard_map/ppermute | solution.py:24
  61.1 4.0 %collective-permute-start.5 = (bf16[128,16,1]{0,2,1:T(2,128)(2,1)S(1)}, bf16[128,16,1]{0,2,1:T(2,128)(2,1)S(1)}, u32[]{:S(2)}, u32[]{:S(2)}) collective-permute-start(bf16[128,16,1]{0,2,1:T(2,128)(2,1)S(1)} %get-tuple-element.26), channel_id=1, source_target_pairs={{4,0},{8,4},{12,8},{0,12},{5,1},{9,5},{13,9},{1,13},{6,2},{10,6},{... | collective-permute-start | bytes 12296 | tf_op jit(solution)/shard_map/ppermute | solution.py:25
  65.1 1.9 %collective-permute-start.6 = (bf16[128,1,130]{0,2,1:T(8,128)(2,1)S(1)}, bf16[128,1,130]{0,2,1:T(8,128)(2,1)S(1)}, u32[]{:S(2)}, u32[]{:S(2)}) collective-permute-start(bf16[128,1,130]{0,2,1:T(8,128)(2,1)S(1)} %get-tuple-element.21), channel_id=1, source_target_pairs={{0,1},{1,0},{2,3},{3,2},{4,5},{5,4},{6,7},{7,6},{8,9},{9,8},{10,11... | collective-permute-start | bytes 99848 | tf_op jit(solution)/shard_map/ppermute | solution.py:24
  65.1 1.9 collective-permute-start.7
  66.7 55.9 %reduce-scatter.2.cloned.1.call-start = ((), (), s32[]{:S(2)}) async-start(), calls=%async_computation.2 | async-start | bytes 3145728 | tf_op jit(solution)/shard_map/reduce_scatter | solution.py:91
  74.1 106.7 %all-reduce.5.cloned.1.call-start = ((), (), s32[]{:S(2)}) async-start(), calls=%async_computation.4 | async-start | bytes 2359296 | tf_op jit(solution)/shard_map/psum | solution.py:10
Sparse Core Ops, SparseCore 0:
  18.3 25.1 all-gather.1
  66.9 20.3 all-reduce.2
  89.6 33.0 reduce-scatter.1
  124.8 55.8 all-reduce.4
